TPU v7x, 32 devices: a whole 2x2x4 slice. The times are simulated.
32 devices in a mesh: ctx: 8 (over z, x), head: 4 (over y, core).
Axes of the slice: x: 2, y: 2, z: 4, core: 2. Of those that a mesh axis runs over, the one named last changes fastest.
Arguments:
- queries: bfloat16 [4096, 4096], P('ctx', 'head'), may hold values from -6 to 6
- key_states: bfloat16 [4096, 4096], P('ctx', 'head'), may hold values from -6 to 6
- value_states: bfloat16 [4096, 4096], P('ctx', 'head'), may hold values from -6 to 6
- transition_vectors: bfloat16 [4096, 4096], P('ctx', 'head'), may hold values from -6 to 6
- beta_logit: float32 [4096, 32], P('ctx', 'head'), may hold values from -6 to 6
- document_ids: int32 [4096], P('ctx'), may hold values from 0 to 7, as said below
- out_weight: bfloat16 [4096, 4096], P('head'), may hold values from -0.09375 to 0.09375
Outputs:
- layer_out: bfloat16 [4096, 4096], P(('ctx', 'head'))
Inputs may be any that keep to these rules, and one draw needn't show every extreme that they name: `document_ids`: document ids never fall along the sequence; document 0 is the first 2304 tokens; the other documents have 1 or more tokens each and together fill the rest.
All inputs are finite; a program needn't handle non-finite values.
Results may differ from a plain program's by a relative error of at most 0.022.
Values may be sent and summed in bfloat16 or wider, within the bound.
No kernel may reach another device: no remote copies, remote signals or barrier semaphores. Data moves between devices by JAX's collectives and lax.ppermute only.
A program may use at most 128 MiB of HBM per device.

v0:
```python
import jax
import jax.numpy as jnp
from jax import lax
from jax.sharding import PartitionSpec as P

epsilon = 1e-06
masked_value = -1e30
highest = lax.Precision.HIGHEST


def shard_operators(query_block, key_block, vector_block, strength):
    block_rows = key_block.shape[0]
    head_width = key_block.shape[1]
    row_ids = jnp.arange(block_rows)
    strict = row_ids[:, None] > row_ids[None, :]
    causal = row_ids[:, None] >= row_ids[None, :]
    intersections = jnp.dot(vector_block, vector_block.T, precision=highest)
    unit_lower = jnp.where(strict, intersections * strength[None, :], 0.0) + jnp.eye(
        block_rows, dtype=jnp.float32
    )
    key_proj = jnp.where(strict, jnp.dot(vector_block, key_block.T, precision=highest), 0.0)
    solved = lax.linalg.triangular_solve(
        unit_lower,
        jnp.concatenate([key_proj, vector_block], axis=1),
        left_side=True,
        lower=True,
        unit_diagonal=True,
    )
    key_solve = solved[:, :block_rows]
    vector_solve = solved[:, block_rows:]
    weighted = strength[:, None] * vector_block
    keys_end = (key_block - jnp.dot(key_solve.T, weighted, precision=highest)).astype(jnp.bfloat16)
    transfer = jnp.eye(head_width, dtype=jnp.float32) - jnp.dot(
        vector_block.T, strength[:, None] * vector_solve, precision=highest
    )
    query_dots = jnp.where(causal, jnp.dot(query_block, vector_block.T, precision=highest), 0.0)
    scaled_dots = query_dots * strength[None, :]
    intra_scores = jnp.dot(query_block, key_block.T, precision=highest) - jnp.dot(
        scaled_dots, key_solve, precision=highest
    )
    rotated = query_block - jnp.dot(scaled_dots, vector_solve, precision=highest)
    return (intra_scores, keys_end, transfer, rotated)


def on_device(
    queries, key_states, value_states, transition_vectors, beta_logit, document_ids, out_weight
):
    block_rows = queries.shape[0]
    head_count = beta_logit.shape[1]
    head_width = queries.shape[1] // head_count
    score_scale = head_width ** (-0.5)

    def split_heads(flat):
        return jnp.transpose(flat.reshape(block_rows, head_count, head_width), (1, 0, 2))

    query_heads = split_heads(queries).astype(jnp.float32)
    key_heads = split_heads(key_states).astype(jnp.float32)
    value_heads = split_heads(value_states)
    vector_heads = split_heads(transition_vectors).astype(jnp.float32)
    unit_vectors = vector_heads / jnp.sqrt(
        jnp.sum(vector_heads * vector_heads, axis=2, keepdims=True) + epsilon
    )
    strength = 2.0 * jax.nn.sigmoid(beta_logit.T)
    intra_scores, keys_end, transfer, rotated = jax.vmap(shard_operators)(
        query_heads, key_heads, unit_vectors, strength
    )
    row_ids = jnp.arange(block_rows)
    causal = row_ids[:, None] >= row_ids[None, :]
    doc_float = (document_ids + 1).astype(jnp.float32)
    same_doc = doc_float[:, None] == doc_float[None, :]
    own_scores = jnp.where((causal & same_doc)[None], intra_scores * score_scale, masked_value)
    running_max = jnp.max(own_scores, axis=2)
    weights = jnp.exp(own_scores - running_max[..., None])
    running_sum = jnp.sum(weights, axis=2)
    accumulated = jnp.einsum(
        "hqk,hkd->hqd",
        weights.astype(jnp.bfloat16),
        value_heads,
        preferred_element_type=jnp.float32,
    )
    ctx_index = lax.axis_index("ctx")
    ctx_count = lax.axis_size("ctx")
    packed = jnp.stack([keys_end, value_heads])

    def attend(carried, key_pair, transfer_in, key_docs, is_live):
        turned, running_max, running_sum, accumulated = carried
        scores = jnp.einsum(
            "hqd,hkd->hqk",
            turned.astype(jnp.bfloat16),
            key_pair[0],
            preferred_element_type=jnp.float32,
        )
        allowed = (doc_float[:, None] == key_docs[None, :]) & is_live
        scores = jnp.where(allowed[None], scores * score_scale, masked_value)
        new_max = jnp.maximum(running_max, jnp.max(scores, axis=2))
        factor = jnp.exp(running_max - new_max)
        weights = jnp.exp(scores - new_max[..., None])
        running_sum = running_sum * factor + jnp.sum(weights, axis=2)
        accumulated = accumulated * factor[..., None] + jnp.einsum(
            "hqk,hkd->hqd",
            weights.astype(jnp.bfloat16),
            key_pair[1],
            preferred_element_type=jnp.float32,
        )
        turned = jnp.einsum("hqd,hde->hqe", turned, transfer_in, precision=highest)
        return (turned, new_max, running_sum, accumulated)

    def visit(carried, key_pair, transfer_in, key_docs, is_live):
        return attend(carried, key_pair, transfer_in, key_docs, is_live)

    carried = (rotated, running_max, running_sum, accumulated)
    every_pair = lax.all_gather(packed, "ctx", axis=2, tiled=True)
    every_transfer, every_doc = (
        lax.all_gather(transfer[None].astype(jnp.bfloat16), "ctx", axis=0, tiled=True).astype(
            jnp.float32
        ),
        lax.all_gather(doc_float.astype(jnp.bfloat16), "ctx", axis=0, tiled=True).astype(
            doc_float.dtype
        ),
    )

    def local_step(offset, inner):
        source = jnp.maximum(ctx_index - offset, 0)
        key_pair = lax.dynamic_slice_in_dim(every_pair, source * block_rows, block_rows, 2)
        transfer_in = lax.dynamic_index_in_dim(every_transfer, source, 0, keepdims=False)
        key_docs = lax.dynamic_slice_in_dim(every_doc, source * block_rows, block_rows, 0)
        return visit(inner, key_pair, transfer_in, key_docs, ctx_index - offset >= 0)

    carried = lax.fori_loop(1, ctx_count, local_step, carried)
    attended = (carried[3] / carried[2][..., None]).astype(jnp.bfloat16)
    token_rows = jnp.transpose(attended, (1, 0, 2)).reshape(block_rows, head_count * head_width)
    return lax.psum_scatter(
        jnp.dot(token_rows, out_weight, preferred_element_type=jnp.float32).astype(jnp.bfloat16),
        "head",
        scatter_dimension=0,
        tiled=True,
    )


def solution(mesh):
    return jax.shard_map(
        on_device,
        mesh=mesh,
        in_specs=(
            P("ctx", "head"),
            P("ctx", "head"),
            P("ctx", "head"),
            P("ctx", "head"),
            P("ctx", "head"),
            P("ctx"),
            P("head", None),
        ),
        out_specs=P(("ctx", "head"), None),
        check_vma=False,
    )
```

profile of v0, /device:TPU:0, one launch (start us, length us, event | category | flops | bytes accessed | tf_op | source)
XLA Modules:
  0.0 895.8 jit_solution(15207088580192670057)
XLA Ops:
  16.1 6.1 broadcast_select_fusion
  22.2 11.6 %select_add_fusion = f32[8,512,512]{1,2,0:T(8,128)} fusion(f32[512,512]{0,1:T(8,128)S(1)} %copy-done.22, f32[512,512]{0,1:T(8,128)S(1)} %copy-done.21, f32[8,512]{1,0:T(8,128)S(1)} %multiply_bitcast_fusion, pred[512,512]{0,1:T(8,128)(4,1)S(1)} %get-tuple-element.265, pred[512,512]{0,1:T(8,128)(4,1)S(1)} %copy-done.23, ...), kind=kOutput, calls=%fused_computation.42 | convolution fusion | flops 3231711232 | bytes 13123584 | tf_op jit(solution)/shard_map/vmap()/dot_general | solution.py:17
  33.8 17.5 %while.21 = (s32[]{:T(128)}, f32[8,512,512]{1,2,0:T(8,128)}, s32[4,2]{0,1:T(2,128)S(1)}, f32[4,8,128,128]{3,2,0,1:T(8,128)}, s32[]{:T(128)}) while((s32[]{:T(128)}, f32[8,512,512]{1,2,0:T(8,128)}, s32[4,2]{0,1:T(2,128)S(1)}, f32[4,8,128,128]{3,2,0,1:T(8,128)}, s32[]{:T(128)}) %tuple.58), condition=%wide.while_cond, body=%wide.while_body.sunk | while | flops 2 | bytes 3145845 | solution.py:22
  51.3 316.0 %custom-call.3 = f32[8,4,128,128]{2,3,1,0:T(8,128)} custom-call(f32[8,4,128,128]{3,2,1,0:T(8,128)} %bitcast.132), custom_call_target="InvertDiagBlocksLowerTriangular" | custom-call | tf_op jit(solution)/shard_map/vmap()/triangular_solve | solution.py:22
  367.4 4.7 fusion.52
  372.1 6.0 fusion.90
  378.1 4.7 fusion.56
  382.9 11.1 %fusion.33 = f32[8,128,640]{1,2,0:T(8,128)S(1)} fusion(f32[8,128,640]{2,1,0:T(8,128)S(1)} %fusion.56, f32[8,128,640]{2,1,0:T(8,128)S(1)} %fusion.52, f32[8,512,512]{1,2,0:T(8,128)} %get-tuple-element.434), kind=kOutput, calls=%fused_computation.54 | convolution fusion | flops 2014576640 | bytes 8912896 | tf_op jit(solution)/shard_map/vmap()/triangular_solve | solution.py:22
  394.0 3.0 fusion.49
  398.6 16.0 %fusion.21 = f32[8,128,640]{1,2,0:T(8,128)} fusion(f32[8,128,640]{2,1,0:T(8,128)S(1)} %fusion.49, f32[8,128,640]{2,1,0:T(8,128)S(1)} %fusion.56, f32[8,128,640]{2,1,0:T(8,128)S(1)} %fusion.52, f32[8,512,512]{1,2,0:T(8,128)} %get-tuple-element.434), kind=kOutput, calls=%fused_computation.43 | convolution fusion | flops 3023831040 | bytes 12058624 | tf_op jit(solution)/shard_map/vmap()/triangular_solve | solution.py:22
  414.6 3.3 copy.108
  417.9 3.3 copy.107
  421.2 3.2 copy.106
  424.4 5.2 fusion.59
  432.5 2.9 fusion.76
  438.4 10.1 %fusion.70 = bf16[1,8,512,128]{3,2,1,0:T(8,128)(2,1)S(1)} fusion(f32[8,512,128]{1,2,0:T(8,128)S(1)} %broadcast_divide_fusion, f32[8,128,640]{1,2,0:T(8,128)} %copy-done.8, f32[8,128,640]{1,2,0:T(8,128)} %copy.108, f32[8,128,640]{1,2,0:T(8,128)} %copy.107, f32[8,128,640]{1,2,0:T(8,128)} %copy.106, bf16[512,8,128]{2,0,1:T(8,128)(2,1)} %copy-done.14, ...), kind=kOutput, calls=%fused_computation.90 | convolution fusion | flops 3229614080 | bytes 14696448 | tf_op jit(solution)/shard_map/vmap()/dot_general | solution.py:32
  454.7 3.6 fusion.84
  458.3 3.3 copy-done.3
  461.6 15.8 %convert_subtract_fusion = f32[8,512,128]{2,1,0:T(8,128)} fusion(f32[8,512,128]{1,2,0:T(8,128)S(1)} %copy-done.7, f32[8,512,512]{2,1,0:T(8,128)S(1)} %fusion.84, f32[8,512]{1,0:T(8,128)S(1)} %multiply_bitcast_fusion, pred[512,512]{0,1:T(8,128)(4,1)S(1)} %iota_compare_fusion.4, bf16[512,8,128]{2,0,1:T(8,128)(2,1)S(1)} %copy.81), kind=kOutput, calls=%fused_computation.88 | convolution fusion | flops 3226468352 | bytes 13910016 | tf_op jit(solution)/shard_map/vmap()/dot_general | solution.py:41
  479.3 28.1 %all-gather.1 = bf16[8,1,512]{2,1,0:T(2,128)(2,1)S(1)} all-gather(bf16[1,1,512]{2,1,0:T(2,128)(2,1)S(1)} %reshape.148), channel_id=1, replica_groups=mesh['ctx'=8,'head'=4] {'ctx'}, dimensions={0}, use_global_device_ids=true | all-gather | bytes 9216 | tf_op jit(solution)/shard_map/all_gather | solution.py:117
  507.6 17.9 %fusion.29 = f32[8,512,512]{1,2,0:T(8,128)S(1)} fusion(f32[8,512,512]{2,1,0:T(8,128)} %copy-done.3, f32[8,512]{1,0:T(8,128)S(1)} %multiply_bitcast_fusion, pred[512,512]{0,1:T(8,128)(4,1)S(1)} %iota_compare_fusion.4, f32[8,128,640]{1,2,0:T(8,128)} %copy-done.8, f32[8,128,640]{1,2,0:T(8,128)} %copy.108, f32[8,128,640]{1,2,0:T(8,128)} %copy.107, ...), kind=kOutput, calls=%fused_computation.51 | convolution fusion | flops 12895387648 | bytes 27541504 | tf_op jit(solution)/shard_map/vmap()/dot_general | solution.py:38
  528.7 3.1 fusion.37
  531.7 4.1 convert.4
  535.9 180.1 %all-gather.5.cloned.1.call-done = bf16[2,8,4096,128]{3,2,1,0:T(8,128)(2,1)} async-done(((bf16[2,8,512,128]{3,2,1,0:T(8,128)(2,1)}), bf16[2,8,4096,128]{3,2,1,0:T(8,128)(2,1)}) %all-gather.5.cloned.1.call-update) | async-done | bytes 16777232 | tf_op jit(solution)/shard_map/all_gather | solution.py:112
  715.9 118.4 %while.20 = (s32[]{:T(128)}, f32[8,512,128]{1,2,0:T(8,128)S(1)}, f32[8,512]{1,0:T(8,128)S(1)}, f32[8,512]{1,0:T(8,128)S(1)}, f32[8,512,128]{2,1,0:T(8,128)}, /*i...) while((s32[]{:T(128)}, f32[8,512,128]{1,2,0:T(8,128)S(1)}, ...), condition=%wide.region_6.7_spmd, body=%wide.region_3.6_spmd.sunk | while | flops 1904222208 | bytes 77340952 | solution.py:129
  716.6 2.8 fusion.125
  719.4 3.4 convolution_bitcast_fusion.2
  724.6 8.4 multiply_add_fusion.5
  733.5 2.8 fusion.125
  736.3 3.4 convolution_bitcast_fusion.2
  741.5 8.4 multiply_add_fusion.5
  750.4 2.8 fusion.125
  753.2 3.4 convolution_bitcast_fusion.2
  758.4 8.4 multiply_add_fusion.5
  767.3 2.8 fusion.125
  770.1 3.4 convolution_bitcast_fusion.2
  775.3 8.4 multiply_add_fusion.5
  784.2 2.8 fusion.125
  786.9 3.4 convolution_bitcast_fusion.2
  792.1 8.4 multiply_add_fusion.5
  801.0 2.8 fusion.125
  803.8 3.4 convolution_bitcast_fusion.2
  809.0 8.4 multiply_add_fusion.5
  817.9 2.8 fusion.125
  820.7 3.4 convolution_bitcast_fusion.2
  825.9 8.4 multiply_add_fusion.5
  836.5 9.5 %convolution_convert_fusion = bf16[512,4096]{1,0:T(8,128)(2,1)} fusion(bf16[512,1024]{0,1:T(8,128)(2,1)S(1)} %bitcast.130, bf16[1024,4096]{1,0:T(8,128)(2,1)} %param.15), kind=kOutput, calls=%fused_computation.53 | convolution fusion | flops 4297064448 | bytes 13631488 | tf_op jit(solution)/shard_map/dot_general | solution.py:133
  846.1 42.9 %reduce-scatter.2.cloned.1.call-done = bf16[128,4096]{1,0:T(8,128)(2,1)} async-done(((bf16[512,4096]{1,0:T(8,128)(2,1)}), bf16[128,4096]{1,0:T(8,128)(2,1)}) %reduce-scatter.2.cloned.1.call-update) | async-done | bytes 1048592 | tf_op jit(solution)/shard_map/reduce_scatter | solution.py:132
  (174 shorter events, 63.8 us)
Async XLA Ops:
  6.5 2.6 copy-start.17
  6.5 525.2 %all-gather.7.cloned.1.call-start = ((), (), s32[]{:S(2)}) async-start(), calls=%async_computation.3 | async-start | bytes 2359296 | tf_op jit(solution)/shard_map/all_gather | solution.py:114
  9.7 1.4 copy-start.5
  11.0 2.0 copy-start.18
  13.0 3.0 copy-start.24
  16.0 6.2 copy-start.14
  16.0 6.1 copy-start.21
  16.0 6.1 copy-start.22
  16.1 6.1 copy-start.23
  367.3 10.7 %copy-start.16 = (f32[8,4,128,128]{2,3,1,0:T(8,128)S(1)}, f32[8,4,128,128]{2,3,1,0:T(8,128)}, u32[]{:S(2)}) copy-start(f32[8,4,128,128]{2,3,1,0:T(8,128)} %custom-call.3) | copy-start | bytes 6291460
  372.1 24.9 %copy-start.1 = (f32[8,128,640]{2,1,0:T(8,128)}, f32[8,128,640]{2,1,0:T(8,128)S(1)}, u32[]{:S(2)}) copy-start(f32[8,128,640]{2,1,0:T(8,128)S(1)} %fusion.52) | copy-start | bytes 7864324
  372.1 21.9 %slice-start = ((s8[8388608]{0:T(1024)(128)(4,1)}), s8[4194304]{0:T(1024)(128)(4,1)S(1)}, s32[]{:S(2)}) async-start(s8[8388608]{0:T(1024)(128)(4,1)} %bitcast.123), calls=%async_computation.4 | async-start | bytes 8388608
  378.1 15.9 %slice-start.1 = ((s8[8388608]{0:T(1024)(128)(4,1)}), s8[4194304]{0:T(1024)(128)(4,1)S(1)}, s32[]{:S(2)}) async-start(s8[8388608]{0:T(1024)(128)(4,1)} %bitcast.123), calls=%async_computation.5 | async-start | bytes 8388608
  382.8 14.1 %copy-start.2 = (f32[8,128,640]{2,1,0:T(8,128)}, f32[8,128,640]{2,1,0:T(8,128)S(1)}, u32[]{:S(2)}) copy-start(f32[8,128,640]{2,1,0:T(8,128)S(1)} %fusion.56) | copy-start | bytes 7864324
  397.0 1.6 copy-start.4
  424.4 5.2 copy-start.9
  424.4 5.2 copy-start.10
  424.4 5.2 copy-start.11
  429.7 1.4 copy-start.8
  431.1 1.4 copy-start.6
  432.5 3.0 copy-start.19
  435.4 280.5 %all-gather.5.cloned.1.call-start = ((), (), s32[]{:S(2)}) async-start(), calls=%async_computation.1 | async-start | bytes 18874368 | tf_op jit(solution)/shard_map/all_gather | solution.py:112
  438.4 10.1 %copy-start.12 = (bf16[512,8,128]{2,0,1:T(8,128)(2,1)}, bf16[512,8,128]{2,0,1:T(8,128)(2,1)S(1)}, u32[]{:S(2)}) copy-start(bf16[512,8,128]{2,0,1:T(8,128)(2,1)S(1)} %copy.114) | copy-start | bytes 3145732
  450.0 1.2 copy-start.20
  450.0 438.9 %reduce-scatter.2.cloned.1.call-start = ((), (), s32[]{:S(2)}) async-start(), calls=%async_computation.2 | async-start | bytes 5242880 | tf_op jit(solution)/shard_map/reduce_scatter | solution.py:132
  454.7 6.9 copy-start.7
  458.3 3.3 copy-start.3
  477.3 1.9 copy-start.25
  507.6 17.9 %copy-start.15 = (bf16[512,8,128]{2,0,1:T(8,128)(2,1)S(1)}, bf16[512,8,128]{2,0,1:T(8,128)(2,1)}, u32[]{:S(2)}) copy-start(bf16[512,8,128]{2,0,1:T(8,128)(2,1)} %copy-done.14) | copy-start | bytes 3145732
  527.4 1.2 copy-start.13
  719.4 5.2 copy-start
  736.3 5.2 copy-start
  753.2 5.2 copy-start
  770.0 5.2 copy-start
  786.9 5.2 copy-start
  803.8 5.2 copy-start
  820.7 5.2 copy-start
Sparse Core Ops, SparseCore 0:
  435.5 51.9 all-gather.6
  489.7 226.1 all-gather.4
  846.2 42.7 reduce-scatter.1
where the time goes:
time: 905 us; the launch traced here: 896 us
  other arithmetic  343 us (38%)
  matrix products  235 us (26%)
  waiting for transfers between devices  223 us (25%)
  local copies, waits for them, and re-layouts  52.5 us (6%)
  blocking collectives  28.1 us (3%)
  between operations  14 us (2%)
    another operation x3, other arithmetic, shard_operators(): lax.linalg.triangular_solve(unit_lower, jnp.concatenate([key_proj, vector...  316 us
    all_gather x1, waiting for transfers between devices, on_device(): every_pair = lax.all_gather(packed, 'ctx', axis=2, tiled=True)  180 us
    dot_general x7, matrix products, attend(): jnp.einsum('hqk,hkd->hqd', weights.astype(jnp.bfloat16), key_pair[1], pre...  58.8 us
    another operation x7, matrix products, shard_operators(): lax.linalg.triangular_solve(unit_lower, jnp.concatenate([key_proj, vector...  50.7 us
    reduce_scatter x1, waiting for transfers between devices, on_device(): lax.psum_scatter(jnp.dot(token_rows, out_weight, preferred_element_type=j...  42.9 us
    all_gather x1, blocking collectives, on_device(): lax.all_gather(doc_float.astype(jnp.bfloat16), 'ctx', axis=0, tiled=True)  28.1 us
    dot_general x7, matrix products, attend(): turned = jnp.einsum('hqd,hde->hqe', turned, transfer_in, precision=highest)  23.7 us
    dot_general x7, matrix products, attend(): jnp.einsum('hqd,hkd->hqk', turned.astype(jnp.bfloat16), key_pair[0], pref...  19.3 us
  transfers between devices with their start and end apart: 3, of which 2 were waited for; matrix products, arithmetic and copies ran while one was open for 8% of the time, Pallas kernels for 0%

commit v1 on v0

--- a/solution.py
+++ b/solution.py
@@ -109,7 +109,12 @@
         return attend(carried, key_pair, transfer_in, key_docs, is_live)
 
     carried = (rotated, running_max, running_sum, accumulated)
-    every_pair = lax.all_gather(packed, "ctx", axis=2, tiled=True)
+    ring = [packed]
+    for hop in range(7):
+        ring.append(lax.ppermute(ring[-1], "ctx", [(dev, (dev + 1) % 8) for dev in range(8)]))
+    every_pair = jnp.roll(
+        jnp.concatenate(ring[::-1], axis=2), (lax.axis_index("ctx") + 1) * ring[0].shape[2], axis=2
+    )
     every_transfer, every_doc = (
         lax.all_gather(transfer[None].astype(jnp.bfloat16), "ctx", axis=0, tiled=True).astype(
             jnp.float32

time: 905 us -> 1060 us (1.17)
  waiting for transfers between devices: 223 us -> 300 us
  blocking collectives: 28.1 us -> 60.9 us
  local copies, waits for them, and re-layouts: 52.5 us -> 81.2 us
    ppermute x0 -> x7, waiting for transfers between devices: none -> 259 us  [on_device(): lax.ppermute(ring[-1], 'ctx', [(dev, (dev + 1) % 8) for dev in range(8)])]
    all_gather x1 -> x0, waiting for transfers between devices: 180 us -> none  [on_device(): every_pair = lax.all_gather(packed, 'ctx', axis=2, tiled=True)]
    all_gather x1, blocking collectives: 28.1 us -> 60.9 us  [on_device(): lax.all_gather(doc_float.astype(jnp.bfloat16), 'ctx', axis=0, tiled=True)]
    unnamed x58 -> x82, local copies, waits for them, and re-layouts: 13.8 us -> 35.6 us
  transfers between devices with their start and end apart: 3 -> 9, of which waited for: 2 -> 6; matrix products, arithmetic and copies ran while one was open for 8% -> 6% of each run, Pallas kernels for 0% -> 0%
where the time goes in v1:
time: 1060 us; the launch traced here: 1050 us
  other arithmetic  342 us (32%)
  waiting for transfers between devices  300 us (28%)
  matrix products  244 us (23%)
  local copies, waits for them, and re-layouts  81.2 us (8%)
  blocking collectives  60.9 us (6%)
  between operations  14.5 us (1%)
    another operation x3, other arithmetic, shard_operators(): lax.linalg.triangular_solve(unit_lower, jnp.concatenate([key_proj, vector...  316 us
    ppermute x7, waiting for transfers between devices, on_device(): lax.ppermute(ring[-1], 'ctx', [(dev, (dev + 1) % 8) for dev in range(8)])  259 us
    all_gather x1, blocking collectives, on_device(): lax.all_gather(doc_float.astype(jnp.bfloat16), 'ctx', axis=0, tiled=True)  60.9 us
    dot_general x7, matrix products, attend(): jnp.einsum('hqk,hkd->hqd', weights.astype(jnp.bfloat16), key_pair[1], pre...  59.1 us
    another operation x7, matrix products, shard_operators(): lax.linalg.triangular_solve(unit_lower, jnp.concatenate([key_proj, vector...  51.7 us
    reduce_scatter x1, waiting for transfers between devices, on_device(): lax.psum_scatter(jnp.dot(token_rows, out_weight, preferred_element_type=j...  41.1 us
    unnamed x82, local copies, waits for them, and re-layouts  35.6 us
    dot_general x7, matrix products, attend(): turned = jnp.einsum('hqd,hde->hqe', turned, transfer_in, precision=highest)  23.7 us
  transfers between devices with their start and end apart: 9, of which 6 were waited for; matrix products, arithmetic and copies ran while one was open for 6% of the time, Pallas kernels for 0%

profile of v1, /device:TPU:0, one launch (start us, length us, event | category | flops | bytes accessed | tf_op | source)
XLA Modules:
  0.0 1046.7 jit_solution(1194075280461022786)
XLA Ops:
  16.1 6.1 broadcast_select_fusion
  22.2 11.6 %select_add_fusion = f32[8,512,512]{1,2,0:T(8,128)} fusion(f32[512,512]{0,1:T(8,128)S(1)} %copy-done.27, f32[512,512]{0,1:T(8,128)S(1)} %copy-done.26, f32[8,512]{1,0:T(8,128)S(1)} %multiply_bitcast_fusion, pred[512,512]{0,1:T(8,128)(4,1)S(1)} %get-tuple-element.265, pred[512,512]{0,1:T(8,128)(4,1)S(1)} %copy-done.28, ...), kind=kOutput, calls=%fused_computation.42 | convolution fusion | flops 3231711232 | bytes 13123584 | tf_op jit(solution)/shard_map/vmap()/dot_general | solution.py:17
  33.8 17.5 %while.21 = (s32[]{:T(128)}, f32[8,512,512]{1,2,0:T(8,128)}, s32[4,2]{0,1:T(2,128)S(1)}, f32[4,8,128,128]{3,2,0,1:T(8,128)}, s32[]{:T(128)}) while((s32[]{:T(128)}, f32[8,512,512]{1,2,0:T(8,128)}, s32[4,2]{0,1:T(2,128)S(1)}, f32[4,8,128,128]{3,2,0,1:T(8,128)}, s32[]{:T(128)}) %tuple.58), condition=%wide.while_cond, body=%wide.while_body.sunk | while | flops 2 | bytes 3145845 | solution.py:22
  51.2 316.0 %custom-call.3 = f32[8,4,128,128]{2,3,1,0:T(8,128)} custom-call(f32[8,4,128,128]{3,2,1,0:T(8,128)} %bitcast.134), custom_call_target="InvertDiagBlocksLowerTriangular" | custom-call | tf_op jit(solution)/shard_map/vmap()/triangular_solve | solution.py:22
  367.3 4.7 fusion.52
  372.0 6.0 fusion.90
  378.0 4.8 fusion.56
  382.8 11.0 %fusion.33 = f32[8,128,640]{1,2,0:T(8,128)S(1)} fusion(f32[8,128,640]{2,1,0:T(8,128)S(1)} %fusion.56, f32[8,128,640]{2,1,0:T(8,128)S(1)} %fusion.52, f32[8,512,512]{1,2,0:T(8,128)} %get-tuple-element.437), kind=kOutput, calls=%fused_computation.54 | convolution fusion | flops 2014576640 | bytes 8912896 | tf_op jit(solution)/shard_map/vmap()/triangular_solve | solution.py:22
  393.9 3.0 fusion.49
  398.4 15.7 %fusion.21 = f32[8,128,640]{1,2,0:T(8,128)} fusion(f32[8,128,640]{2,1,0:T(8,128)S(1)} %fusion.49, f32[8,128,640]{2,1,0:T(8,128)S(1)} %fusion.56, f32[8,128,640]{2,1,0:T(8,128)S(1)} %fusion.52, f32[8,512,512]{1,2,0:T(8,128)} %get-tuple-element.437), kind=kOutput, calls=%fused_computation.43 | convolution fusion | flops 3023831040 | bytes 12058624 | tf_op jit(solution)/shard_map/vmap()/triangular_solve | solution.py:22
  414.1 3.2 copy.108
  417.3 3.3 copy.107
  420.6 3.2 copy.106
  423.8 6.5 fusion.59
  433.3 10.1 fusion.70
  443.6 3.0 collective-permute-start
  446.6 48.7 %collective-permute-done = bf16[2,8,512,128]{3,2,1,0:T(8,128)(2,1)S(1)} collective-permute-done((bf16[2,8,512,128]{3,2,1,0:T(8,128)(2,1)S(1)}, bf16[2,8,512,128]{3,2,1,0:T(8,128)(2,1)S(1)}, u32[]{:S(2)}, u32[]{:S(2)}) %collective-permute-start) | collective-permute-done | bytes 2097184 | tf_op jit(solution)/shard_map/ppermute | solution.py:114
  495.3 49.5 %collective-permute-done.1 = bf16[2,8,512,128]{3,2,1,0:T(8,128)(2,1)S(1)} collective-permute-done((bf16[2,8,512,128]{3,2,1,0:T(8,128)(2,1)S(1)}, bf16[2,8,512,128]{3,2,1,0:T(8,128)(2,1)S(1)}, u32[]{:S(2)}, u32[]{:S(2)}) %collective-permute-start.1) | collective-permute-done | bytes 2097184 | tf_op jit(solution)/shard_map/ppermute | solution.py:114
  546.1 48.6 %collective-permute-done.2 = bf16[2,8,512,128]{3,2,1,0:T(8,128)(2,1)S(1)} collective-permute-done((bf16[2,8,512,128]{3,2,1,0:T(8,128)(2,1)S(1)}, bf16[2,8,512,128]{3,2,1,0:T(8,128)(2,1)S(1)}, u32[]{:S(2)}, u32[]{:S(2)}) %collective-permute-start.2) | collective-permute-done | bytes 2097184 | tf_op jit(solution)/shard_map/ppermute | solution.py:114
  596.0 47.8 %collective-permute-done.3 = bf16[2,8,512,128]{3,2,1,0:T(8,128)(2,1)} collective-permute-done((bf16[2,8,512,128]{3,2,1,0:T(8,128)(2,1)S(1)}, bf16[2,8,512,128]{3,2,1,0:T(8,128)(2,1)}, u32[]{:S(2)}, u32[]{:S(2)}) %collective-permute-start.3) | collective-permute-done | bytes 2097184 | tf_op jit(solution)/shard_map/ppermute | solution.py:114
  645.4 2.9 fusion.76
  653.0 64.8 %collective-permute-done.4 = bf16[2,8,512,128]{3,2,1,0:T(8,128)(2,1)} collective-permute-done((bf16[2,8,512,128]{3,2,1,0:T(8,128)(2,1)}, bf16[2,8,512,128]{3,2,1,0:T(8,128)(2,1)}, u32[]{:S(2)}, u32[]{:S(2)}) %collective-permute-start.4) | collective-permute-done | bytes 2097184 | tf_op jit(solution)/shard_map/ppermute | solution.py:114
  718.2 4.8 fusion.84
  723.1 3.3 copy-done.3
  726.3 15.8 %convert_subtract_fusion = f32[8,512,128]{2,1,0:T(8,128)} fusion(f32[8,512,128]{1,2,0:T(8,128)S(1)} %copy-done.7, f32[8,512,512]{2,1,0:T(8,128)S(1)} %fusion.84, f32[8,512]{1,0:T(8,128)S(1)} %multiply_bitcast_fusion, pred[512,512]{0,1:T(8,128)(4,1)S(1)} %iota_compare_fusion.4, bf16[512,8,128]{2,0,1:T(8,128)(2,1)S(1)} %copy-done.8), kind=kOutput, calls=%fused_computation.88 | convolution fusion | flops 3226468352 | bytes 13910016 | tf_op jit(solution)/shard_map/vmap()/dot_general | solution.py:41
  744.1 20.2 %fusion.29 = f32[8,512,512]{1,2,0:T(8,128)} fusion(f32[8,512,512]{2,1,0:T(8,128)} %copy-done.3, f32[8,512]{1,0:T(8,128)S(1)} %multiply_bitcast_fusion, pred[512,512]{0,1:T(8,128)(4,1)S(1)} %iota_compare_fusion.4, f32[8,128,640]{1,2,0:T(8,128)} %fusion.59, f32[8,128,640]{1,2,0:T(8,128)} %copy.108, f32[8,128,640]{1,2,0:T(8,128)} %copy.107, ...), kind=kOutput, calls=%fused_computation.51 | convolution fusion | flops 12895387648 | bytes 27541504 | tf_op jit(solution)/shard_map/vmap()/dot_general | solution.py:38
  764.3 60.9 %all-gather.1 = bf16[8,1,512]{2,1,0:T(2,128)(2,1)S(1)} all-gather(bf16[1,1,512]{2,1,0:T(2,128)(2,1)S(1)} %reshape.148), channel_id=1, replica_groups=mesh['ctx'=8,'head'=4] {'ctx'}, dimensions={0}, use_global_device_ids=true | all-gather | bytes 9216 | tf_op jit(solution)/shard_map/all_gather | solution.py:122
  825.5 5.9 fusion.105
  832.6 3.1 fusion.37
  835.7 4.1 convert.4
  861.2 6.9 constant_dynamic-slice_fusion.2
  868.1 118.4 %while.20 = (s32[]{:T(128)}, f32[8,512,128]{1,2,0:T(8,128)S(1)}, f32[8,512]{1,0:T(8,128)S(1)}, f32[8,512]{1,0:T(8,128)S(1)}, f32[8,512,128]{2,1,0:T(8,128)}, /*i...) while((s32[]{:T(128)}, f32[8,512,128]{1,2,0:T(8,128)S(1)}, ...), condition=%wide.region_6.7_spmd, body=%wide.region_3.6_spmd.sunk | while | flops 1904222208 | bytes 77340952 | solution.py:134
  871.4 3.4 convolution_bitcast_fusion.2
  876.6 8.4 multiply_add_fusion.5
  888.3 3.4 convolution_bitcast_fusion.2
  893.5 8.4 multiply_add_fusion.5
  905.2 3.4 convolution_bitcast_fusion.2
  910.4 8.4 multiply_add_fusion.5
  922.1 3.4 convolution_bitcast_fusion.2
  927.3 8.4 multiply_add_fusion.5
  939.1 3.4 convolution_bitcast_fusion.2
  944.3 8.4 multiply_add_fusion.5
  956.0 3.4 convolution_bitcast_fusion.2
  961.2 8.4 multiply_add_fusion.5
  972.9 3.4 convolution_bitcast_fusion.2
  978.1 8.4 multiply_add_fusion.5
  988.8 9.5 convolution_convert_fusion
  998.3 41.1 %reduce-scatter.2.cloned.1.call-done = bf16[128,4096]{1,0:T(8,128)(2,1)} async-done(((bf16[512,4096]{1,0:T(8,128)(2,1)}), bf16[128,4096]{1,0:T(8,128)(2,1)}) %reduce-scatter.2.cloned.1.call-update) | async-done | bytes 1048592 | tf_op jit(solution)/shard_map/reduce_scatter | solution.py:137
  (212 shorter events, 102.7 us)
Async XLA Ops:
  6.5 2.6 copy-start.23
  6.5 829.2 %all-gather.4.cloned.1.call-start = ((), (), s32[]{:S(2)}) async-start(), calls=%async_computation.2 | async-start | bytes 2359296 | tf_op jit(solution)/shard_map/all_gather | solution.py:119
  9.7 1.4 copy-start.5
  11.0 2.0 copy-start.24
  13.0 3.0 copy-start.29
  16.0 6.2 copy-start.15
  16.0 6.2 copy-start.26
  16.0 6.2 copy-start.27
  16.1 6.1 copy-start.28
  367.3 10.7 %copy-start.22 = (f32[8,4,128,128]{2,3,1,0:T(8,128)S(1)}, f32[8,4,128,128]{2,3,1,0:T(8,128)}, u32[]{:S(2)}) copy-start(f32[8,4,128,128]{2,3,1,0:T(8,128)} %custom-call.3) | copy-start | bytes 6291460
  372.0 24.8 %copy-start.1 = (f32[8,128,640]{2,1,0:T(8,128)}, f32[8,128,640]{2,1,0:T(8,128)S(1)}, u32[]{:S(2)}) copy-start(f32[8,128,640]{2,1,0:T(8,128)S(1)} %fusion.52) | copy-start | bytes 7864324
  372.0 21.8 %slice-start = ((s8[8388608]{0:T(1024)(128)(4,1)}), s8[4194304]{0:T(1024)(128)(4,1)S(1)}, s32[]{:S(2)}) async-start(s8[8388608]{0:T(1024)(128)(4,1)} %bitcast.123), calls=%async_computation.3 | async-start | bytes 8388608
  378.0 15.8 %slice-start.1 = ((s8[8388608]{0:T(1024)(128)(4,1)}), s8[4194304]{0:T(1024)(128)(4,1)S(1)}, s32[]{:S(2)}) async-start(s8[8388608]{0:T(1024)(128)(4,1)} %bitcast.123), calls=%async_computation.4 | async-start | bytes 8388608
  382.8 14.1 %copy-start.2 = (f32[8,128,640]{2,1,0:T(8,128)}, f32[8,128,640]{2,1,0:T(8,128)S(1)}, u32[]{:S(2)}) copy-start(f32[8,128,640]{2,1,0:T(8,128)S(1)} %fusion.56) | copy-start | bytes 7864324
  396.9 1.5 copy-start.4
  423.8 6.5 copy-start.25
  433.3 210.5 %copy-start.10 = (f32[8,128,640]{1,2,0:T(8,128)S(1)}, f32[8,128,640]{1,2,0:T(8,128)}, u32[]{:S(2)}) copy-start(f32[8,128,640]{1,2,0:T(8,128)} %copy.108) | copy-start | bytes 7864324
  433.3 210.5 %copy-start.11 = (f32[8,128,640]{1,2,0:T(8,128)S(1)}, f32[8,128,640]{1,2,0:T(8,128)}, u32[]{:S(2)}) copy-start(f32[8,128,640]{1,2,0:T(8,128)} %copy.107) | copy-start | bytes 7864324
  433.3 210.5 %copy-start.12 = (f32[8,128,640]{1,2,0:T(8,128)S(1)}, f32[8,128,640]{1,2,0:T(8,128)}, u32[]{:S(2)}) copy-start(f32[8,128,640]{1,2,0:T(8,128)} %copy.106) | copy-start | bytes 7864324
  443.4 200.6 %copy-start.13 = (bf16[1,8,512,128]{3,2,1,0:T(8,128)(2,1)}, bf16[1,8,512,128]{3,2,1,0:T(8,128)(2,1)S(1)}, u32[]{:S(2)}) copy-start(bf16[1,8,512,128]{3,2,1,0:T(8,128)(2,1)S(1)} %fusion.70) | copy-start | bytes 3145732
  443.4 200.4 %copy-start.9 = (f32[8,128,640]{1,2,0:T(8,128)S(1)}, f32[8,128,640]{1,2,0:T(8,128)}, u32[]{:S(2)}) copy-start(f32[8,128,640]{1,2,0:T(8,128)} %fusion.59) | copy-start | bytes 7864324
  443.6 51.7 %collective-permute-start = (bf16[2,8,512,128]{3,2,1,0:T(8,128)(2,1)S(1)}, bf16[2,8,512,128]{3,2,1,0:T(8,128)(2,1)S(1)}, u32[]{:S(2)}, u32[]{:S(2)}) collective-permute-start(bf16[2,8,512,128]{3,2,1,0:T(8,128)(2,1)S(1)} %pad_maximum_fusion.7), channel_id=1, source_target_pairs={{0,4},{4,8},{8,12},{12,16},{16,20},{20,24},{24,28},{28,0},{1,5},{5... | collective-permute-start | bytes 6291464 | tf_op jit(solution)/shard_map/ppermute | solution.py:114
  495.3 148.7 %copy-start.16 = (bf16[2,8,512,128]{3,2,1,0:T(8,128)(2,1)}, bf16[2,8,512,128]{3,2,1,0:T(8,128)(2,1)S(1)}, u32[]{:S(2)}) copy-start(bf16[2,8,512,128]{3,2,1,0:T(8,128)(2,1)S(1)} %collective-permute-done) | copy-start | bytes 6291460
  495.3 49.5 %collective-permute-start.1 = (bf16[2,8,512,128]{3,2,1,0:T(8,128)(2,1)S(1)}, bf16[2,8,512,128]{3,2,1,0:T(8,128)(2,1)S(1)}, u32[]{:S(2)}, u32[]{:S(2)}) collective-permute-start(bf16[2,8,512,128]{3,2,1,0:T(8,128)(2,1)S(1)} %collective-permute-done), channel_id=1, source_target_pairs={{0,4},{4,8},{8,12},{12,16},{16,20},{20,24},{24,28},{28,0},{1,5},{5... | collective-permute-start | bytes 6291464 | tf_op jit(solution)/shard_map/ppermute | solution.py:114
  544.8 1.3 copy-start.18
  546.1 48.6 %collective-permute-start.2 = (bf16[2,8,512,128]{3,2,1,0:T(8,128)(2,1)S(1)}, bf16[2,8,512,128]{3,2,1,0:T(8,128)(2,1)S(1)}, u32[]{:S(2)}, u32[]{:S(2)}) collective-permute-start(bf16[2,8,512,128]{3,2,1,0:T(8,128)(2,1)S(1)} %collective-permute-done.1), channel_id=1, source_target_pairs={{0,4},{4,8},{8,12},{12,16},{16,20},{20,24},{24,28},{28,0},{1,5},{5... | collective-permute-start | bytes 6291464 | tf_op jit(solution)/shard_map/ppermute | solution.py:114
  594.7 1.3 copy-start.20
  596.0 47.8 %collective-permute-start.3 = (bf16[2,8,512,128]{3,2,1,0:T(8,128)(2,1)S(1)}, bf16[2,8,512,128]{3,2,1,0:T(8,128)(2,1)}, u32[]{:S(2)}, u32[]{:S(2)}) collective-permute-start(bf16[2,8,512,128]{3,2,1,0:T(8,128)(2,1)S(1)} %collective-permute-done.2), channel_id=1, source_target_pairs={{0,4},{4,8},{8,12},{12,16},{16,20},{20,24},{24,28},{28,0},{1,5},{5... | collective-permute-start | bytes 6291464 | tf_op jit(solution)/shard_map/ppermute | solution.py:114
  643.8 74.0 %collective-permute-start.4 = (bf16[2,8,512,128]{3,2,1,0:T(8,128)(2,1)}, bf16[2,8,512,128]{3,2,1,0:T(8,128)(2,1)}, u32[]{:S(2)}, u32[]{:S(2)}) collective-permute-start(bf16[2,8,512,128]{3,2,1,0:T(8,128)(2,1)} %collective-permute-done.3), channel_id=1, source_target_pairs={{0,4},{4,8},{8,12},{12,16},{16,20},{20,24},{24,28},{28,0},{1,5},{5... | collective-permute-start | bytes 6291464 | tf_op jit(solution)/shard_map/ppermute | solution.py:114
  644.0 1.4 copy-start.6
  648.3 391.1 %reduce-scatter.2.cloned.1.call-start = ((), (), s32[]{:S(2)}) async-start(), calls=%async_computation.1 | async-start | bytes 5242880 | tf_op jit(solution)/shard_map/reduce_scatter | solution.py:137
  653.0 73.4 %copy-start.7 = (f32[8,512,128]{1,2,0:T(8,128)S(1)}, f32[8,512,128]{1,2,0:T(8,128)}, u32[]{:S(2)}) copy-start(f32[8,512,128]{1,2,0:T(8,128)} %copy-done.6) | copy-start | bytes 6291460
  653.0 73.4 %copy-start.8 = (bf16[512,8,128]{2,0,1:T(8,128)(2,1)S(1)}, bf16[512,8,128]{2,0,1:T(8,128)(2,1)}, u32[]{:S(2)}) copy-start(bf16[512,8,128]{2,0,1:T(8,128)(2,1)} %copy.81) | copy-start | bytes 3145732
  717.8 46.5 %collective-permute-start.5 = (bf16[2,8,512,128]{3,2,1,0:T(8,128)(2,1)}, bf16[2,8,512,128]{3,2,1,0:T(8,128)(2,1)}, u32[]{:S(2)}, u32[]{:S(2)}) collective-permute-start(bf16[2,8,512,128]{3,2,1,0:T(8,128)(2,1)} %collective-permute-done.4), channel_id=1, source_target_pairs={{0,4},{4,8},{8,12},{12,16},{16,20},{20,24},{24,28},{28,0},{1,5},{5... | collective-permute-start | bytes 6291464 | tf_op jit(solution)/shard_map/ppermute | solution.py:114
  723.0 3.3 copy-start.3
  744.1 20.2 %copy-start.30 = (s32[512]{0:T(512)S(1)}, s32[512]{0:T(512)}, u32[]{:S(2)}) copy-start(s32[512]{0:T(512)} %param.14) | copy-start | bytes 6148
  764.3 75.5 %collective-permute-start.6 = (bf16[2,8,512,128]{3,2,1,0:T(8,128)(2,1)}, bf16[2,8,512,128]{3,2,1,0:T(8,128)(2,1)}, u32[]{:S(2)}, u32[]{:S(2)}) collective-permute-start(bf16[2,8,512,128]{3,2,1,0:T(8,128)(2,1)} %collective-permute-done.5), channel_id=1, source_target_pairs={{0,4},{4,8},{8,12},{12,16},{16,20},{20,24},{24,28},{28,0},{1,5},{5... | collective-permute-start | bytes 6291464 | tf_op jit(solution)/shard_map/ppermute | solution.py:114
  845.4 2.2 copy-start.21
  847.7 1.6 copy-start.19
  849.2 1.6 copy-start.17
  850.8 1.2 copy-start.14
  871.4 5.2 copy-start
  888.3 5.2 copy-start
  905.2 5.2 copy-start
  922.1 5.2 copy-start
  939.0 5.2 copy-start
  956.0 5.2 copy-start
  972.9 5.2 copy-start
Sparse Core Ops, SparseCore 0:
  648.4 66.3 all-gather.3
  998.4 40.9 reduce-scatter.1
